TPU v7x, 512 devices: a whole 4x8x8 slice. The times are simulated.
512 devices in a mesh: heads: 8 (over y), ctx: 64 (over z, x, core).
Axes of the slice: x: 4, y: 8, z: 8, core: 2. Of those that a mesh axis runs over, the one named last changes fastest.
Arguments:
- queries: bfloat16 [16384, 4096], P('ctx', 'heads'), may hold values from -6 to 6
- keys: bfloat16 [16384, 1024], P('ctx', 'heads'), may hold values from -6 to 6
- values: bfloat16 [16384, 1024], P('ctx', 'heads'), may hold values from -6 to 6
- out_weight: bfloat16 [4096, 4096], P('heads'), may hold values from -0.09375 to 0.09375
- out_grad: bfloat16 [4096, 16384], P('heads', 'ctx'), may hold values from -6 to 6
- doc_lengths: int32 [16], replicated, may hold values from 1 to 1792, 16384 in all
Outputs:
- out_t: bfloat16 [4096, 16384], P('heads', 'ctx')
- grad_q: bfloat16 [16384, 4096], P('ctx', 'heads')
- grad_k: bfloat16 [16384, 1024], P('ctx', 'heads')
- grad_v: bfloat16 [16384, 1024], P('ctx', 'heads')
Inputs may be any that keep to these rules, and one draw needn't show every extreme that they name: `doc_lengths`: the 16 lengths sum to 16384; the longest document has exactly 1792 tokens.
All inputs are finite; a program needn't handle non-finite values.
Results may differ from a plain program's by a relative error of at most 0.02.
Values may be sent and summed in bfloat16 or wider, within the bound.
No kernel may reach another device: no remote copies, remote signals or barrier semaphores. Data moves between devices by JAX's collectives and lax.ppermute only.
A program may use at most 64 MiB of HBM per device.

v0:
```python
import math
import jax
import jax.numpy as jnp
from jax import lax
from jax.sharding import PartitionSpec as P

REACH = 7


def passed_along(value, axis, steps):
    count = lax.axis_size(axis)
    first, last = (max(0, -steps), min(count, count - steps))
    return lax.ppermute(value, axis, [(source, source + steps) for source in range(first, last)])


def per_device(queries, keys, values, out_weight, out_grad, doc_lengths):
    tok_rows = queries.shape[0]
    head_dim = keys.shape[1]
    group_size = queries.shape[1] // head_dim
    scaling = 1.0 / math.sqrt(head_dim)
    shard = lax.axis_index("ctx")
    doc_ends = jnp.cumsum(doc_lengths)
    starts = doc_ends - doc_lengths
    positions = shard * tok_rows + jnp.arange(tok_rows, dtype=jnp.int32)
    first_key = jnp.max(
        jnp.where(starts[None, :] <= positions[:, None], starts[None, :], 0), axis=1
    )
    stacked = jnp.concatenate([keys, values], axis=1)
    blocks = [stacked[None]]
    for offset in range(1, REACH + 1):
        blocks.append(passed_along(stacked, "ctx", offset)[None])
    window = jnp.concatenate(blocks, axis=0)
    num_blocks = window.shape[0]
    flat_keys = window[:, :, :head_dim].reshape(num_blocks * tok_rows, head_dim)
    flat_values = window[:, :, head_dim:].reshape(num_blocks * tok_rows, head_dim)
    key_pos = (
        (shard - jnp.arange(num_blocks, dtype=jnp.int32))[:, None] * tok_rows
        + jnp.arange(tok_rows, dtype=jnp.int32)[None, :]
    ).reshape(-1)
    visible = (key_pos[None, :] >= first_key[:, None]) & (key_pos[None, :] <= positions[:, None])
    query_heads = queries.reshape(tok_rows, group_size, head_dim)
    scores = (
        jnp.einsum("tgd,kd->gtk", query_heads, flat_keys, preferred_element_type=jnp.float32)
        * scaling
    )
    scores = jnp.where(visible[None], scores, -jnp.inf)
    largest = jnp.max(scores, axis=-1, keepdims=True)
    expons = jnp.exp(scores - largest)
    weights = expons / jnp.sum(expons, axis=-1, keepdims=True)
    probs = weights.astype(jnp.bfloat16)
    attn_heads = jnp.einsum(
        "gtk,kd->tgd", probs, flat_values, preferred_element_type=jnp.float32
    ).astype(jnp.bfloat16)
    attn = attn_heads.reshape(tok_rows, group_size * head_dim)
    columns = out_weight
    out_t = lax.psum_scatter(
        lax.dot_general(
            columns, attn, (((0,), (1,)), ((), ())), preferred_element_type=jnp.float32
        ),
        "heads",
        scatter_dimension=0,
        tiled=True,
    ).astype(jnp.bfloat16)
    columns = out_weight
    grad_attn = jnp.dot(
        columns,
        lax.all_gather(out_grad, "heads", axis=0, tiled=True),
        preferred_element_type=jnp.float32,
    ).astype(jnp.bfloat16)
    grad_heads = grad_attn.reshape(group_size, head_dim, tok_rows)
    delta_sum = jnp.einsum(
        "tgd,gdt->gt", attn_heads, grad_heads, preferred_element_type=jnp.float32
    )
    grad_probs = jnp.einsum(
        "gdt,kd->gtk", grad_heads, flat_values, preferred_element_type=jnp.float32
    )
    dscore = (weights * (grad_probs - delta_sum[:, :, None]) * scaling).astype(jnp.bfloat16)
    grad_q = (
        jnp.einsum("gtk,kd->tgd", dscore, flat_keys, preferred_element_type=jnp.float32)
        .astype(jnp.bfloat16)
        .reshape(tok_rows, group_size * head_dim)
    )
    key_part = jnp.einsum("gtk,tgd->kd", dscore, query_heads, preferred_element_type=jnp.float32)
    value_part = jnp.einsum("gtk,gdt->kd", probs, grad_heads, preferred_element_type=jnp.float32)
    partial_grads = jnp.concatenate([key_part, value_part], axis=1).reshape(
        num_blocks, tok_rows, 2 * head_dim
    )
    summed = partial_grads[0]
    for offset in range(1, num_blocks):
        summed = summed + passed_along(partial_grads[offset], "ctx", -offset)
    grad_k = summed[:, :head_dim].astype(jnp.bfloat16)
    grad_v = summed[:, head_dim:].astype(jnp.bfloat16)
    return (out_t, grad_q, grad_k, grad_v)


def solution(mesh):
    placed = (
        P("ctx", "heads"),
        P("ctx", "heads"),
        P("ctx", "heads"),
        P("heads", None),
        P("heads", "ctx"),
        P(),
    )
    return jax.shard_map(
        per_device,
        mesh=mesh,
        in_specs=placed,
        out_specs=(P("heads", "ctx"), P("ctx", "heads"), P("ctx", "heads"), P("ctx", "heads")),
        check_vma=False,
    )
```

profile of v0, /device:TPU:10, one launch (start us, length us, event | category | flops | bytes accessed | tf_op | source)
XLA Modules:
  0.0 153.6 jit_solution(13572130763276567545)
XLA Ops:
  8.9 3.7 %collective-permute-start.6 = (bf16[256,256]{1,0:T(8,128)(2,1)S(1)}, bf16[256,256]{1,0:T(8,128)(2,1)S(1)}, u32[]{:S(2)}, u32[]{:S(2)}) collective-permute-start(bf16[256,256]{1,0:T(8,128)(2,1)S(1)} %constant_dynamic-update-slice_fusion), channel_id=1, source_target_pairs={{0,7},{1,8},{2,9},{3,10},{4,11},{5,12},{6,13},{7,14},{8,15},{9,16}... | collective-permute-start | bytes 393224 | tf_op jit(solution)/shard_map/ppermute | solution.py:13
  12.6 4.7 %collective-permute-start.5 = (bf16[256,256]{1,0:T(8,128)(2,1)S(1)}, bf16[256,256]{1,0:T(8,128)(2,1)S(1)}, u32[]{:S(2)}, u32[]{:S(2)}) collective-permute-start(bf16[256,256]{1,0:T(8,128)(2,1)S(1)} %constant_dynamic-update-slice_fusion), channel_id=1, source_target_pairs={{0,6},{1,7},{2,8},{3,9},{4,10},{5,11},{6,12},{7,13},{8,14},{9,15},... | collective-permute-start | bytes 393224 | tf_op jit(solution)/shard_map/ppermute | solution.py:13
  17.3 3.9 %collective-permute-start.4 = (bf16[256,256]{1,0:T(8,128)(2,1)S(1)}, bf16[256,256]{1,0:T(8,128)(2,1)S(1)}, u32[]{:S(2)}, u32[]{:S(2)}) collective-permute-start(bf16[256,256]{1,0:T(8,128)(2,1)S(1)} %constant_dynamic-update-slice_fusion), channel_id=1, source_target_pairs={{0,5},{1,6},{2,7},{3,8},{4,9},{5,10},{6,11},{7,12},{8,13},{9,14},{... | collective-permute-start | bytes 393224 | tf_op jit(solution)/shard_map/ppermute | solution.py:13
  21.3 4.8 %collective-permute-start.3 = (bf16[256,256]{1,0:T(8,128)(2,1)S(1)}, bf16[256,256]{1,0:T(8,128)(2,1)S(1)}, u32[]{:S(2)}, u32[]{:S(2)}) collective-permute-start(bf16[256,256]{1,0:T(8,128)(2,1)S(1)} %constant_dynamic-update-slice_fusion), channel_id=1, source_target_pairs={{0,4},{1,5},{2,6},{3,7},{4,8},{5,9},{6,10},{7,11},{8,12},{9,13},{1... | collective-permute-start | bytes 393224 | tf_op jit(solution)/shard_map/ppermute | solution.py:13
  26.1 1.9 %collective-permute-start = (bf16[256,256]{1,0:T(8,128)(2,1)S(1)}, bf16[256,256]{1,0:T(8,128)(2,1)S(1)}, u32[]{:S(2)}, u32[]{:S(2)}) collective-permute-start(bf16[256,256]{1,0:T(8,128)(2,1)S(1)} %constant_dynamic-update-slice_fusion), channel_id=1, source_target_pairs={{0,1},{1,2},{2,3},{3,4},{4,5},{5,6},{6,7},{7,8},{8,9},{9,10},{10,1... | collective-permute-start | bytes 393224 | tf_op jit(solution)/shard_map/ppermute | solution.py:13
  30.4 1.1 copy.75
  32.4 3.4 %collective-permute-start.1 = (bf16[256,256]{1,0:T(8,128)(2,1)S(1)}, bf16[256,256]{1,0:T(8,128)(2,1)S(1)}, u32[]{:S(2)}, u32[]{:S(2)}) collective-permute-start(bf16[256,256]{1,0:T(8,128)(2,1)S(1)} %constant_dynamic-update-slice_fusion), channel_id=1, source_target_pairs={{0,2},{1,3},{2,4},{3,5},{4,6},{5,7},{6,8},{7,9},{8,10},{9,11},{10,... | collective-permute-start | bytes 393224 | tf_op jit(solution)/shard_map/ppermute | solution.py:13
  35.8 4.6 %collective-permute-done.1 = bf16[256,256]{1,0:T(8,128)(2,1)S(1)} collective-permute-done((bf16[256,256]{1,0:T(8,128)(2,1)S(1)}, bf16[256,256]{1,0:T(8,128)(2,1)S(1)}, u32[]{:S(2)}, u32[]{:S(2)}) %collective-permute-start.1) | collective-permute-done | bytes 131104 | tf_op jit(solution)/shard_map/ppermute | solution.py:13
  40.4 2.9 %collective-permute-start.2 = (bf16[256,256]{1,0:T(8,128)(2,1)S(1)}, bf16[256,256]{1,0:T(8,128)(2,1)S(1)}, u32[]{:S(2)}, u32[]{:S(2)}) collective-permute-start(bf16[256,256]{1,0:T(8,128)(2,1)S(1)} %constant_dynamic-update-slice_fusion), channel_id=1, source_target_pairs={{0,3},{1,4},{2,5},{3,6},{4,7},{5,8},{6,9},{7,10},{8,11},{9,12},{10... | collective-permute-start | bytes 393224 | tf_op jit(solution)/shard_map/ppermute | solution.py:13
  43.4 2.5 %collective-permute-done.2 = bf16[256,256]{1,0:T(8,128)(2,1)S(1)} collective-permute-done((bf16[256,256]{1,0:T(8,128)(2,1)S(1)}, bf16[256,256]{1,0:T(8,128)(2,1)S(1)}, u32[]{:S(2)}, u32[]{:S(2)}) %collective-permute-start.2) | collective-permute-done | bytes 131104 | tf_op jit(solution)/shard_map/ppermute | solution.py:13
  46.3 4.8 %fusion.28 = (f32[4,256]{1,0:T(4,128)S(1)}, f32[4,256,2048]{1,2,0:T(8,128)}) fusion(pred[256,2048]{0,1:T(8,128)(4,1)S(1)} %compare_and_fusion, bf16[2048,128,1]{1,0,2:T(8,128)(2,1)S(1)} %bitcast.79, bf16[256,4,128]{0,2,1:T(8,128)(2,1)S(1)} %bitcast.86), kind=kOutput, calls=%fused_computation.68 | convolution fusion | flops 545261568 | bytes 9703424 | tf_op jit(solution)/shard_map/sub | solution.py:48
  51.1 6.0 %fusion.5 = bf16[4,256,2048]{1,2,0:T(8,128)(2,1)} fusion(f32[4,256,2048]{1,2,0:T(8,128)} %get-tuple-element.28, f32[4,256]{1,0:T(4,128)S(1)} %get-tuple-element.27), kind=kLoop, calls=%fused_computation.24 | loop fusion | flops 4194304 | bytes 12587008 | tf_op jit(solution)/shard_map/convert_element_type | solution.py:50
  57.1 18.4 %all-gather.2.cloned.1.call-done = bf16[4096,256]{1,0:T(8,128)(2,1)} async-done(((bf16[512,256]{1,0:T(8,128)(2,1)}), bf16[4096,256]{1,0:T(8,128)(2,1)}) %all-gather.2.cloned.1.call-update) | async-done | bytes 2097168 | tf_op jit(solution)/shard_map/all_gather | solution.py:67
  75.6 4.2 %convolution_convert_fusion = bf16[512,256]{1,0:T(8,128)(2,1)S(1)} fusion(bf16[512,4096]{1,0:T(8,128)(2,1)} %param.9, bf16[4096,256]{1,0:T(8,128)(2,1)} %all-gather.2.cloned.1.call-done), kind=kOutput, calls=%fused_computation.28 | convolution fusion | flops 1073872896 | bytes 6553600 | tf_op jit(solution)/shard_map/dot_general | solution.py:65
  80.7 1.4 copy-done.1
  82.0 3.3 %convolution_bitcast_fusion = f32[4096,256]{0,1:T(8,128)} fusion(bf16[256,512]{0,1:T(8,128)(2,1)S(1)} %bitcast.83, bf16[512,4096]{1,0:T(8,128)(2,1)S(1)} %copy-done.1), kind=kOutput, calls=%fused_computation.5 | convolution fusion | flops 1073741824 | bytes 8650752 | tf_op jit(solution)/shard_map/dot_general | solution.py:57
  85.3 3.6 %convolution_bitcast_fusion.1 = f32[2048,128]{0,1:T(8,128)S(1)} fusion(bf16[4,256,2048]{1,2,0:T(8,128)(2,1)} %fusion.5, bf16[4,128,256]{2,1,0:T(8,128)(2,1)S(1)} %bitcast.84), kind=kOutput, calls=%fused_computation.25 | convolution fusion | flops 536870912 | bytes 5505024 | tf_op jit(solution)/shard_map/gtk,gdt->kd/dot_general | solution.py:84
  89.0 4.3 %multiply_convert_fusion = bf16[4,256,2048]{1,2,0:T(8,128)(2,1)S(1)} fusion(bf16[2048,128,1]{1,0,2:T(8,128)(2,1)S(1)} %bitcast.82, bf16[4,128,256]{2,1,0:T(8,128)(2,1)S(1)} %bitcast.85, f32[4,256]{1,0:T(4,128)S(1)} %get-tuple-element.29, f32[4,256,2048]{1,2,0:T(8,128)} %get-tuple-element.28, f32[4,256]{1,0:T(4,128)S(1)} %get-tuple-element.27), kind=kOutput, calls=%fused_computation.2 | convolution fusion | flops 547356672 | bytes 13377536 | tf_op jit(solution)/shard_map/gdt,kd->gtk/dot_general | solution.py:74
  93.3 1.5 convolution_bitcast_fusion.2
  95.9 1.9 %collective-permute-start.7 = (f32[256,256]{0,1:T(8,128)S(1)}, f32[256,256]{0,1:T(8,128)S(1)}, u32[]{:S(2)}, u32[]{:S(2)}) collective-permute-start(f32[256,256]{0,1:T(8,128)S(1)} %get-tuple-element.16), channel_id=1, source_target_pairs={{1,0},{2,1},{3,2},{4,3},{5,4},{6,5},{7,6},{8,7},{9,8},{10,9},{11,1... | collective-permute-start | bytes 786440 | tf_op jit(solution)/shard_map/ppermute | solution.py:13
  97.8 1.9 %collective-permute-start.8 = (f32[256,256]{0,1:T(8,128)S(1)}, f32[256,256]{0,1:T(8,128)S(1)}, u32[]{:S(2)}, u32[]{:S(2)}) collective-permute-start(f32[256,256]{0,1:T(8,128)S(1)} %get-tuple-element.17), channel_id=1, source_target_pairs={{2,0},{3,1},{4,2},{5,3},{6,4},{7,5},{8,6},{9,7},{10,8},{11,9},{12,... | collective-permute-start | bytes 786440 | tf_op jit(solution)/shard_map/ppermute | solution.py:13
  99.7 1.3 collective-permute-start.9
  101.0 1.3 collective-permute-start.10
  102.3 1.3 collective-permute-start.11
  103.7 1.3 collective-permute-start.13
  105.0 5.1 %collective-permute-done.8 = f32[256,256]{0,1:T(8,128)S(1)} collective-permute-done((f32[256,256]{0,1:T(8,128)S(1)}, f32[256,256]{0,1:T(8,128)S(1)}, u32[]{:S(2)}, u32[]{:S(2)}) %collective-permute-start.8) | collective-permute-done | bytes 262176 | tf_op jit(solution)/shard_map/ppermute | solution.py:13
  110.0 1.3 collective-permute-start.12
  113.7 8.1 %collective-permute-done.10 = f32[256,256]{0,1:T(8,128)} collective-permute-done((f32[256,256]{0,1:T(8,128)}, f32[256,256]{0,1:T(8,128)}, u32[]{:S(2)}, u32[]{:S(2)}) %collective-permute-start.10) | collective-permute-done | bytes 262176 | tf_op jit(solution)/shard_map/ppermute | solution.py:13
  121.8 2.3 %collective-permute-done.11 = f32[256,256]{0,1:T(8,128)} collective-permute-done((f32[256,256]{0,1:T(8,128)}, f32[256,256]{0,1:T(8,128)}, u32[]{:S(2)}, u32[]{:S(2)}) %collective-permute-start.11) | collective-permute-done | bytes 262176 | tf_op jit(solution)/shard_map/ppermute | solution.py:13
  124.1 11.9 %collective-permute-done.13 = f32[256,256]{0,1:T(8,128)} collective-permute-done((f32[256,256]{0,1:T(8,128)}, f32[256,256]{0,1:T(8,128)}, u32[]{:S(2)}, u32[]{:S(2)}) %collective-permute-start.13) | collective-permute-done | bytes 262176 | tf_op jit(solution)/shard_map/ppermute | solution.py:13
  135.9 6.0 %collective-permute-done.12 = f32[256,256]{0,1:T(8,128)} collective-permute-done((f32[256,256]{0,1:T(8,128)}, f32[256,256]{0,1:T(8,128)}, u32[]{:S(2)}, u32[]{:S(2)}) %collective-permute-start.12) | collective-permute-done | bytes 262176 | tf_op jit(solution)/shard_map/ppermute | solution.py:13
  142.0 1.4 fusion.23
  (45 shorter events, 13.0 us)
Async XLA Ops:
  7.2 68.4 %all-gather.2.cloned.1.call-start = ((), (), s32[]{:S(2)}) async-start(), calls=%async_computation.2 | async-start | bytes 2359296 | tf_op jit(solution)/shard_map/all_gather | solution.py:67
  8.9 37.0 %collective-permute-start.6 = (bf16[256,256]{1,0:T(8,128)(2,1)S(1)}, bf16[256,256]{1,0:T(8,128)(2,1)S(1)}, u32[]{:S(2)}, u32[]{:S(2)}) collective-permute-start(bf16[256,256]{1,0:T(8,128)(2,1)S(1)} %constant_dynamic-update-slice_fusion), channel_id=1, source_target_pairs={{0,7},{1,8},{2,9},{3,10},{4,11},{5,12},{6,13},{7,14},{8,15},{9,16}... | collective-permute-start | bytes 393224 | tf_op jit(solution)/shard_map/ppermute | solution.py:13
  12.6 33.3 %collective-permute-start.5 = (bf16[256,256]{1,0:T(8,128)(2,1)S(1)}, bf16[256,256]{1,0:T(8,128)(2,1)S(1)}, u32[]{:S(2)}, u32[]{:S(2)}) collective-permute-start(bf16[256,256]{1,0:T(8,128)(2,1)S(1)} %constant_dynamic-update-slice_fusion), channel_id=1, source_target_pairs={{0,6},{1,7},{2,8},{3,9},{4,10},{5,11},{6,12},{7,13},{8,14},{9,15},... | collective-permute-start | bytes 393224 | tf_op jit(solution)/shard_map/ppermute | solution.py:13
  17.3 28.6 %collective-permute-start.4 = (bf16[256,256]{1,0:T(8,128)(2,1)S(1)}, bf16[256,256]{1,0:T(8,128)(2,1)S(1)}, u32[]{:S(2)}, u32[]{:S(2)}) collective-permute-start(bf16[256,256]{1,0:T(8,128)(2,1)S(1)} %constant_dynamic-update-slice_fusion), channel_id=1, source_target_pairs={{0,5},{1,6},{2,7},{3,8},{4,9},{5,10},{6,11},{7,12},{8,13},{9,14},{... | collective-permute-start | bytes 393224 | tf_op jit(solution)/shard_map/ppermute | solution.py:13
  21.3 24.6 %collective-permute-start.3 = (bf16[256,256]{1,0:T(8,128)(2,1)S(1)}, bf16[256,256]{1,0:T(8,128)(2,1)S(1)}, u32[]{:S(2)}, u32[]{:S(2)}) collective-permute-start(bf16[256,256]{1,0:T(8,128)(2,1)S(1)} %constant_dynamic-update-slice_fusion), channel_id=1, source_target_pairs={{0,4},{1,5},{2,6},{3,7},{4,8},{5,9},{6,10},{7,11},{8,12},{9,13},{1... | collective-permute-start | bytes 393224 | tf_op jit(solution)/shard_map/ppermute | solution.py:13
  26.1 6.3 %collective-permute-start = (bf16[256,256]{1,0:T(8,128)(2,1)S(1)}, bf16[256,256]{1,0:T(8,128)(2,1)S(1)}, u32[]{:S(2)}, u32[]{:S(2)}) collective-permute-start(bf16[256,256]{1,0:T(8,128)(2,1)S(1)} %constant_dynamic-update-slice_fusion), channel_id=1, source_target_pairs={{0,1},{1,2},{2,3},{3,4},{4,5},{5,6},{6,7},{7,8},{8,9},{9,10},{10,1... | collective-permute-start | bytes 393224 | tf_op jit(solution)/shard_map/ppermute | solution.py:13
  28.0 116.8 %reduce-scatter.2.cloned.1.call-start = ((), (), s32[]{:S(2)}) async-start(), calls=%async_computation.1 | async-start | bytes 4718592 | tf_op jit(solution)/shard_map/reduce_scatter | solution.py:56
  32.4 8.1 %collective-permute-start.1 = (bf16[256,256]{1,0:T(8,128)(2,1)S(1)}, bf16[256,256]{1,0:T(8,128)(2,1)S(1)}, u32[]{:S(2)}, u32[]{:S(2)}) collective-permute-start(bf16[256,256]{1,0:T(8,128)(2,1)S(1)} %constant_dynamic-update-slice_fusion), channel_id=1, source_target_pairs={{0,2},{1,3},{2,4},{3,5},{4,6},{5,7},{6,8},{7,9},{8,10},{9,11},{10,... | collective-permute-start | bytes 393224 | tf_op jit(solution)/shard_map/ppermute | solution.py:13
  40.4 5.4 %collective-permute-start.2 = (bf16[256,256]{1,0:T(8,128)(2,1)S(1)}, bf16[256,256]{1,0:T(8,128)(2,1)S(1)}, u32[]{:S(2)}, u32[]{:S(2)}) collective-permute-start(bf16[256,256]{1,0:T(8,128)(2,1)S(1)} %constant_dynamic-update-slice_fusion), channel_id=1, source_target_pairs={{0,3},{1,4},{2,5},{3,6},{4,7},{5,8},{6,9},{7,10},{8,11},{9,12},{10... | collective-permute-start | bytes 393224 | tf_op jit(solution)/shard_map/ppermute | solution.py:13
  75.6 4.3 %copy-start = (bf16[4,256,2048]{1,2,0:T(8,128)(2,1)S(1)}, bf16[4,256,2048]{1,2,0:T(8,128)(2,1)}, u32[]{:S(2)}) copy-start(bf16[4,256,2048]{1,2,0:T(8,128)(2,1)} %fusion.5) | copy-start | bytes 12582916
  79.8 2.2 %copy-start.1 = (bf16[512,4096]{1,0:T(8,128)(2,1)S(1)}, bf16[512,4096]{1,0:T(8,128)(2,1)}, u32[]{:S(2)}) copy-start(bf16[512,4096]{1,0:T(8,128)(2,1)} %param.9) | copy-start | bytes 12582916
  95.9 7.7 %collective-permute-start.7 = (f32[256,256]{0,1:T(8,128)S(1)}, f32[256,256]{0,1:T(8,128)S(1)}, u32[]{:S(2)}, u32[]{:S(2)}) collective-permute-start(f32[256,256]{0,1:T(8,128)S(1)} %get-tuple-element.16), channel_id=1, source_target_pairs={{1,0},{2,1},{3,2},{4,3},{5,4},{6,5},{7,6},{8,7},{9,8},{10,9},{11,1... | collective-permute-start | bytes 786440 | tf_op jit(solution)/shard_map/ppermute | solution.py:13
  97.8 12.2 %collective-permute-start.8 = (f32[256,256]{0,1:T(8,128)S(1)}, f32[256,256]{0,1:T(8,128)S(1)}, u32[]{:S(2)}, u32[]{:S(2)}) collective-permute-start(f32[256,256]{0,1:T(8,128)S(1)} %get-tuple-element.17), channel_id=1, source_target_pairs={{2,0},{3,1},{4,2},{5,3},{6,4},{7,5},{8,6},{9,7},{10,8},{11,9},{12,... | collective-permute-start | bytes 786440 | tf_op jit(solution)/shard_map/ppermute | solution.py:13
  99.7 14.0 %collective-permute-start.9 = (f32[256,256]{0,1:T(8,128)}, f32[256,256]{0,1:T(8,128)}, u32[]{:S(2)}, u32[]{:S(2)}) collective-permute-start(f32[256,256]{0,1:T(8,128)} %get-tuple-element.18), channel_id=1, source_target_pairs={{3,0},{4,1},{5,2},{6,3},{7,4},{8,5},{9,6},{10,7},{11,8},{12,9},{13... | collective-permute-start | bytes 786440 | tf_op jit(solution)/shard_map/ppermute | solution.py:13
  101.0 20.8 %collective-permute-start.10 = (f32[256,256]{0,1:T(8,128)}, f32[256,256]{0,1:T(8,128)}, u32[]{:S(2)}, u32[]{:S(2)}) collective-permute-start(f32[256,256]{0,1:T(8,128)} %get-tuple-element.19), channel_id=1, source_target_pairs={{4,0},{5,1},{6,2},{7,3},{8,4},{9,5},{10,6},{11,7},{12,8},{13,9},{1... | collective-permute-start | bytes 786440 | tf_op jit(solution)/shard_map/ppermute | solution.py:13
  102.3 21.7 %collective-permute-start.11 = (f32[256,256]{0,1:T(8,128)}, f32[256,256]{0,1:T(8,128)}, u32[]{:S(2)}, u32[]{:S(2)}) collective-permute-start(f32[256,256]{0,1:T(8,128)} %get-tuple-element.20), channel_id=1, source_target_pairs={{5,0},{6,1},{7,2},{8,3},{9,4},{10,5},{11,6},{12,7},{13,8},{14,9},{... | collective-permute-start | bytes 786440 | tf_op jit(solution)/shard_map/ppermute | solution.py:13
  103.7 32.3 %collective-permute-start.13 = (f32[256,256]{0,1:T(8,128)}, f32[256,256]{0,1:T(8,128)}, u32[]{:S(2)}, u32[]{:S(2)}) collective-permute-start(f32[256,256]{0,1:T(8,128)} %get-tuple-element.21), channel_id=1, source_target_pairs={{7,0},{8,1},{9,2},{10,3},{11,4},{12,5},{13,6},{14,7},{15,8},{16,9}... | collective-permute-start | bytes 786440 | tf_op jit(solution)/shard_map/ppermute | solution.py:13
  110.0 32.0 %collective-permute-start.12 = (f32[256,256]{0,1:T(8,128)}, f32[256,256]{0,1:T(8,128)}, u32[]{:S(2)}, u32[]{:S(2)}) collective-permute-start(f32[256,256]{0,1:T(8,128)} %get-tuple-element.22), channel_id=1, source_target_pairs={{6,0},{7,1},{8,2},{9,3},{10,4},{11,5},{12,6},{13,7},{14,8},{15,9},... | collective-permute-start | bytes 786440 | tf_op jit(solution)/shard_map/ppermute | solution.py:13
Sparse Core Ops, SparseCore 0:
  28.2 47.3 all-gather.1
  85.5 55.6 reduce-scatter.1
where the time goes:
time: 154 us
  waiting for transfers between devices  60.6 us (39%)
  starting transfers between devices  35.7 us (23%)
  matrix products  23.4 us (15%)
  between operations  14.4 us (9%)
  other arithmetic  11.1 us (7%)
  local copies, waits for them, and re-layouts  8.43 us (5%)
    ppermute x14, waiting for transfers between devices, passed_along(): lax.ppermute(value, axis, [(source, source + steps) for source in range(f...  42.1 us
    ppermute x14, starting transfers between devices, passed_along(): lax.ppermute(value, axis, [(source, source + steps) for source in range(f...  35.6 us
    all_gather x1, waiting for transfers between devices, per_device(): lax.all_gather(out_grad, 'heads', axis=0, tiled=True)  18.4 us
    convert_element_type x1, other arithmetic, per_device(): probs = weights.astype(jnp.bfloat16)  6.04 us
    unnamed x17, local copies, waits for them, and re-layouts  5.47 us
    sub x1, matrix products, per_device(): expons = jnp.exp(scores - largest)  4.84 us
    dot_general x1, matrix products, per_device(): jnp.einsum('gdt,kd->gtk', grad_heads, flat_values, preferred_element_type...  4.34 us
    dot_general x1, matrix products, per_device(): jnp.dot(columns, lax.all_gather(out_grad, 'heads', axis=0, tiled=True), p...  4.25 us
  transfers between devices with their start and end apart: 16, of which 10 were waited for; matrix products, arithmetic and copies ran while one was open for 19% of the time, Pallas kernels for 0%

commit v1 on v0

--- a/solution.py
+++ b/solution.py
@@ -5,6 +5,11 @@
 from jax.sharding import PartitionSpec as P
 
 REACH = 7
+
+
+def swapped_in(x, axis, dim):
+    sent = jnp.stack([x] * lax.axis_size(axis))
+    return jnp.concatenate(lax.all_to_all(sent, axis, 0, 0), axis=dim)
 
 
 def passed_along(value, axis, steps):
@@ -63,9 +68,7 @@
     ).astype(jnp.bfloat16)
     columns = out_weight
     grad_attn = jnp.dot(
-        columns,
-        lax.all_gather(out_grad, "heads", axis=0, tiled=True),
-        preferred_element_type=jnp.float32,
+        columns, swapped_in(out_grad, "heads", 0), preferred_element_type=jnp.float32
     ).astype(jnp.bfloat16)
     grad_heads = grad_attn.reshape(group_size, head_dim, tok_rows)
     delta_sum = jnp.einsum(

time: 154 us -> 174 us (1.13)
  the two profiles are of different devices: /device:TPU:10 before, /device:TPU:66 now
where the time goes in v1:
time: 174 us; the launch traced here: 173 us
  waiting for transfers between devices  65.2 us (37%)
  starting transfers between devices  49.8 us (29%)
  matrix products  23.6 us (14%)
  between operations  14.4 us (8%)
  other arithmetic  11.2 us (6%)
  local copies, waits for them, and re-layouts  9.34 us (5%)
    ppermute x14, waiting for transfers between devices, passed_along(): lax.ppermute(value, axis, [(source, source + steps) for source in range(f...  43.6 us
    ppermute x14, starting transfers between devices, passed_along(): lax.ppermute(value, axis, [(source, source + steps) for source in range(f...  42.6 us
    all_to_all x1, waiting for transfers between devices, swapped_in(): return jnp.concatenate(lax.all_to_all(sent, axis, 0, 0), axis=dim)  21.6 us
    all_to_all x1, starting transfers between devices, swapped_in(): return jnp.concatenate(lax.all_to_all(sent, axis, 0, 0), axis=dim)  7.1 us
    convert_element_type x1, other arithmetic, per_device(): probs = weights.astype(jnp.bfloat16)  6.01 us
    sub x1, matrix products, per_device(): expons = jnp.exp(scores - largest)  5.74 us
    unnamed x25, local copies, waits for them, and re-layouts  5.54 us
    dot_general x1, matrix products, per_device(): jnp.einsum('gdt,kd->gtk', grad_heads, flat_values, preferred_element_type...  4.37 us
  transfers between devices with their start and end apart: 16, of which 8 were waited for; matrix products, arithmetic and copies ran while one was open for 18% of the time, Pallas kernels for 0%

profile of v1, /device:TPU:66, one launch (start us, length us, event | category | flops | bytes accessed | tf_op | source)
XLA Modules:
  0.0 173.5 jit_solution(7016793121162407497)
XLA Ops:
  8.9 3.7 %collective-permute-start.6 = (bf16[256,256]{1,0:T(8,128)(2,1)S(1)}, bf16[256,256]{1,0:T(8,128)(2,1)S(1)}, u32[]{:S(2)}, u32[]{:S(2)}) collective-permute-start(bf16[256,256]{1,0:T(8,128)(2,1)S(1)} %constant_dynamic-update-slice_fusion), channel_id=1, source_target_pairs={{0,7},{1,8},{2,9},{3,10},{4,11},{5,12},{6,13},{7,14},{8,15},{9,16}... | collective-permute-start | bytes 393224 | tf_op jit(solution)/shard_map/ppermute | solution.py:18
  12.6 4.7 %collective-permute-start.5 = (bf16[256,256]{1,0:T(8,128)(2,1)S(1)}, bf16[256,256]{1,0:T(8,128)(2,1)S(1)}, u32[]{:S(2)}, u32[]{:S(2)}) collective-permute-start(bf16[256,256]{1,0:T(8,128)(2,1)S(1)} %constant_dynamic-update-slice_fusion), channel_id=1, source_target_pairs={{0,6},{1,7},{2,8},{3,9},{4,10},{5,11},{6,12},{7,13},{8,14},{9,15},... | collective-permute-start | bytes 393224 | tf_op jit(solution)/shard_map/ppermute | solution.py:18
  17.3 3.9 %collective-permute-start.4 = (bf16[256,256]{1,0:T(8,128)(2,1)S(1)}, bf16[256,256]{1,0:T(8,128)(2,1)S(1)}, u32[]{:S(2)}, u32[]{:S(2)}) collective-permute-start(bf16[256,256]{1,0:T(8,128)(2,1)S(1)} %constant_dynamic-update-slice_fusion), channel_id=1, source_target_pairs={{0,5},{1,6},{2,7},{3,8},{4,9},{5,10},{6,11},{7,12},{8,13},{9,14},{... | collective-permute-start | bytes 393224 | tf_op jit(solution)/shard_map/ppermute | solution.py:18
  21.3 6.0 %collective-permute-start.3 = (bf16[256,256]{1,0:T(8,128)(2,1)S(1)}, bf16[256,256]{1,0:T(8,128)(2,1)S(1)}, u32[]{:S(2)}, u32[]{:S(2)}) collective-permute-start(bf16[256,256]{1,0:T(8,128)(2,1)S(1)} %constant_dynamic-update-slice_fusion), channel_id=1, source_target_pairs={{0,4},{1,5},{2,6},{3,7},{4,8},{5,9},{6,10},{7,11},{8,12},{9,13},{1... | collective-permute-start | bytes 393224 | tf_op jit(solution)/shard_map/ppermute | solution.py:18
  27.3 1.9 %collective-permute-start = (bf16[256,256]{1,0:T(8,128)(2,1)S(1)}, bf16[256,256]{1,0:T(8,128)(2,1)S(1)}, u32[]{:S(2)}, u32[]{:S(2)}) collective-permute-start(bf16[256,256]{1,0:T(8,128)(2,1)S(1)} %constant_dynamic-update-slice_fusion), channel_id=1, source_target_pairs={{0,1},{1,2},{2,3},{3,4},{4,5},{5,6},{6,7},{7,8},{8,9},{9,10},{10,1... | collective-permute-start | bytes 393224 | tf_op jit(solution)/shard_map/ppermute | solution.py:18
  29.2 2.4 %stack.2 = bf16[8,512,256]{2,1,0:T(8,128)(2,1)} broadcast(bf16[512,256]{1,0:T(8,128)(2,1)} %param.10), dimensions={1,2} | broadcast | bytes 2359296 | tf_op jit(solution)/shard_map/stack | solution.py:11
  31.7 7.1 %all-to-all-start = ((bf16[8,512,256]{2,1,0:T(8,128)(2,1)}), bf16[8,512,256]{2,1,0:T(8,128)(2,1)S(1)}, u32[]{:S(2)}, u32[]{:S(2)}) async-start(bf16[8,512,256]{2,1,0:T(8,128)(2,1)} %stack.2), calls=%async_computation.1 | async-start | bytes 4194304 | tf_op jit(solution)/shard_map/all_to_all | solution.py:12
  40.8 3.4 %collective-permute-start.1 = (bf16[256,256]{1,0:T(8,128)(2,1)S(1)}, bf16[256,256]{1,0:T(8,128)(2,1)S(1)}, u32[]{:S(2)}, u32[]{:S(2)}) collective-permute-start(bf16[256,256]{1,0:T(8,128)(2,1)S(1)} %constant_dynamic-update-slice_fusion), channel_id=1, source_target_pairs={{0,2},{1,3},{2,4},{3,5},{4,6},{5,7},{6,8},{7,9},{8,10},{9,11},{10,... | collective-permute-start | bytes 393224 | tf_op jit(solution)/shard_map/ppermute | solution.py:18
  44.2 4.5 %collective-permute-done.1 = bf16[256,256]{1,0:T(8,128)(2,1)S(1)} collective-permute-done((bf16[256,256]{1,0:T(8,128)(2,1)S(1)}, bf16[256,256]{1,0:T(8,128)(2,1)S(1)}, u32[]{:S(2)}, u32[]{:S(2)}) %collective-permute-start.1) | collective-permute-done | bytes 131104 | tf_op jit(solution)/shard_map/ppermute | solution.py:18
  48.7 3.5 %collective-permute-start.2 = (bf16[256,256]{1,0:T(8,128)(2,1)S(1)}, bf16[256,256]{1,0:T(8,128)(2,1)S(1)}, u32[]{:S(2)}, u32[]{:S(2)}) collective-permute-start(bf16[256,256]{1,0:T(8,128)(2,1)S(1)} %constant_dynamic-update-slice_fusion), channel_id=1, source_target_pairs={{0,3},{1,4},{2,5},{3,6},{4,7},{5,8},{6,9},{7,10},{8,11},{9,12},{10... | collective-permute-start | bytes 393224 | tf_op jit(solution)/shard_map/ppermute | solution.py:18
  52.2 5.5 %collective-permute-done.2 = bf16[256,256]{1,0:T(8,128)(2,1)S(1)} collective-permute-done((bf16[256,256]{1,0:T(8,128)(2,1)S(1)}, bf16[256,256]{1,0:T(8,128)(2,1)S(1)}, u32[]{:S(2)}, u32[]{:S(2)}) %collective-permute-start.2) | collective-permute-done | bytes 131104 | tf_op jit(solution)/shard_map/ppermute | solution.py:18
  58.1 5.7 %fusion.28 = (f32[4,256]{1,0:T(4,128)S(1)}, f32[4,256,2048]{1,2,0:T(8,128)}) fusion(pred[256,2048]{0,1:T(8,128)(4,1)} %compare_and_fusion, bf16[2048,128,1]{1,0,2:T(8,128)(2,1)S(1)} %bitcast.81, bf16[256,4,128]{0,2,1:T(8,128)(2,1)S(1)} %bitcast.88), kind=kOutput, calls=%fused_computation.68 | convolution fusion | flops 545261568 | bytes 9703424 | tf_op jit(solution)/shard_map/sub | solution.py:53
  63.9 6.0 %fusion.5 = bf16[4,256,2048]{1,2,0:T(8,128)(2,1)} fusion(f32[4,256,2048]{1,2,0:T(8,128)} %get-tuple-element.28, f32[4,256]{1,0:T(4,128)S(1)} %get-tuple-element.27), kind=kLoop, calls=%fused_computation.24 | loop fusion | flops 4194304 | bytes 12587008 | tf_op jit(solution)/shard_map/convert_element_type | solution.py:55
  69.9 21.6 %all-to-all-done = bf16[8,512,256]{2,1,0:T(8,128)(2,1)S(1)} async-done(((bf16[8,512,256]{2,1,0:T(8,128)(2,1)}), bf16[8,512,256]{2,1,0:T(8,128)(2,1)S(1)}, u32[]{:S(2)}, u32[]{:S(2)}) %all-to-all-start) | async-done | bytes 2097184 | tf_op jit(solution)/shard_map/all_to_all | solution.py:12
  91.4 3.6 %convolution_convert_fusion = bf16[512,256]{1,0:T(8,128)(2,1)S(1)} fusion(bf16[512,4096]{1,0:T(8,128)(2,1)} %param.9, bf16[4096,256]{1,0:T(8,128)(2,1)S(1)} %bitcast.80), kind=kOutput, calls=%fused_computation.28 | convolution fusion | flops 1073872896 | bytes 6553600 | tf_op jit(solution)/shard_map/dot_general | solution.py:70
  95.9 1.4 copy-done.1
  97.2 3.3 %convolution_bitcast_fusion = f32[4096,256]{0,1:T(8,128)} fusion(bf16[256,512]{0,1:T(8,128)(2,1)S(1)} %bitcast.85, bf16[512,4096]{1,0:T(8,128)(2,1)S(1)} %copy-done.1), kind=kOutput, calls=%fused_computation.5 | convolution fusion | flops 1073741824 | bytes 8650752 | tf_op jit(solution)/shard_map/dot_general | solution.py:62
  100.5 3.7 %convolution_bitcast_fusion.1 = f32[2048,128]{0,1:T(8,128)S(1)} fusion(bf16[4,256,2048]{1,2,0:T(8,128)(2,1)} %fusion.5, bf16[4,128,256]{2,1,0:T(8,128)(2,1)S(1)} %bitcast.86), kind=kOutput, calls=%fused_computation.25 | convolution fusion | flops 536870912 | bytes 5505024 | tf_op jit(solution)/shard_map/gtk,gdt->kd/dot_general | solution.py:87
  104.2 4.4 %multiply_convert_fusion = bf16[4,256,2048]{1,2,0:T(8,128)(2,1)S(1)} fusion(bf16[2048,128,1]{1,0,2:T(8,128)(2,1)S(1)} %bitcast.84, bf16[4,128,256]{2,1,0:T(8,128)(2,1)S(1)} %bitcast.87, f32[4,256]{1,0:T(4,128)S(1)} %get-tuple-element.29, f32[4,256,2048]{1,2,0:T(8,128)} %get-tuple-element.28, f32[4,256]{1,0:T(4,128)S(1)} %get-tuple-element.27), kind=kOutput, calls=%fused_computation.2 | convolution fusion | flops 547356672 | bytes 13377536 | tf_op jit(solution)/shard_map/gdt,kd->gtk/dot_general | solution.py:77
  108.6 1.5 convolution_bitcast_fusion.2
  111.1 1.9 %collective-permute-start.7 = (f32[256,256]{0,1:T(8,128)S(1)}, f32[256,256]{0,1:T(8,128)S(1)}, u32[]{:S(2)}, u32[]{:S(2)}) collective-permute-start(f32[256,256]{0,1:T(8,128)S(1)} %get-tuple-element.16), channel_id=1, source_target_pairs={{1,0},{2,1},{3,2},{4,3},{5,4},{6,5},{7,6},{8,7},{9,8},{10,9},{11,1... | collective-permute-start | bytes 786440 | tf_op jit(solution)/shard_map/ppermute | solution.py:18
  113.1 3.4 %collective-permute-start.8 = (f32[256,256]{0,1:T(8,128)S(1)}, f32[256,256]{0,1:T(8,128)S(1)}, u32[]{:S(2)}, u32[]{:S(2)}) collective-permute-start(f32[256,256]{0,1:T(8,128)S(1)} %get-tuple-element.17), channel_id=1, source_target_pairs={{2,0},{3,1},{4,2},{5,3},{6,4},{7,5},{8,6},{9,7},{10,8},{11,9},{12,... | collective-permute-start | bytes 786440 | tf_op jit(solution)/shard_map/ppermute | solution.py:18
  116.5 1.9 %collective-permute-start.9 = (f32[256,256]{0,1:T(8,128)}, f32[256,256]{0,1:T(8,128)}, u32[]{:S(2)}, u32[]{:S(2)}) collective-permute-start(f32[256,256]{0,1:T(8,128)} %get-tuple-element.18), channel_id=1, source_target_pairs={{3,0},{4,1},{5,2},{6,3},{7,4},{8,5},{9,6},{10,7},{11,8},{12,9},{13... | collective-permute-start | bytes 786440 | tf_op jit(solution)/shard_map/ppermute | solution.py:18
  118.4 2.5 %collective-permute-start.10 = (f32[256,256]{0,1:T(8,128)}, f32[256,256]{0,1:T(8,128)}, u32[]{:S(2)}, u32[]{:S(2)}) collective-permute-start(f32[256,256]{0,1:T(8,128)} %get-tuple-element.19), channel_id=1, source_target_pairs={{4,0},{5,1},{6,2},{7,3},{8,4},{9,5},{10,6},{11,7},{12,8},{13,9},{1... | collective-permute-start | bytes 786440 | tf_op jit(solution)/shard_map/ppermute | solution.py:18
  120.9 1.9 %collective-permute-start.11 = (f32[256,256]{0,1:T(8,128)}, f32[256,256]{0,1:T(8,128)}, u32[]{:S(2)}, u32[]{:S(2)}) collective-permute-start(f32[256,256]{0,1:T(8,128)} %get-tuple-element.20), channel_id=1, source_target_pairs={{5,0},{6,1},{7,2},{8,3},{9,4},{10,5},{11,6},{12,7},{13,8},{14,9},{... | collective-permute-start | bytes 786440 | tf_op jit(solution)/shard_map/ppermute | solution.py:18
  122.9 1.9 %collective-permute-start.13 = (f32[256,256]{0,1:T(8,128)}, f32[256,256]{0,1:T(8,128)}, u32[]{:S(2)}, u32[]{:S(2)}) collective-permute-start(f32[256,256]{0,1:T(8,128)} %get-tuple-element.21), channel_id=1, source_target_pairs={{7,0},{8,1},{9,2},{10,3},{11,4},{12,5},{13,6},{14,7},{15,8},{16,9}... | collective-permute-start | bytes 786440 | tf_op jit(solution)/shard_map/ppermute | solution.py:18
  125.7 1.9 %collective-permute-start.12 = (f32[256,256]{0,1:T(8,128)}, f32[256,256]{0,1:T(8,128)}, u32[]{:S(2)}, u32[]{:S(2)}) collective-permute-start(f32[256,256]{0,1:T(8,128)} %get-tuple-element.22), channel_id=1, source_target_pairs={{6,0},{7,1},{8,2},{9,3},{10,4},{11,5},{12,6},{13,7},{14,8},{15,9},... | collective-permute-start | bytes 786440 | tf_op jit(solution)/shard_map/ppermute | solution.py:18
  129.3 8.8 %collective-permute-done.10 = f32[256,256]{0,1:T(8,128)} collective-permute-done((f32[256,256]{0,1:T(8,128)}, f32[256,256]{0,1:T(8,128)}, u32[]{:S(2)}, u32[]{:S(2)}) %collective-permute-start.10) | collective-permute-done | bytes 262176 | tf_op jit(solution)/shard_map/ppermute | solution.py:18
  138.1 5.1 %collective-permute-done.11 = f32[256,256]{0,1:T(8,128)} collective-permute-done((f32[256,256]{0,1:T(8,128)}, f32[256,256]{0,1:T(8,128)}, u32[]{:S(2)}, u32[]{:S(2)}) %collective-permute-start.11) | collective-permute-done | bytes 262176 | tf_op jit(solution)/shard_map/ppermute | solution.py:18
  143.1 12.1 %collective-permute-done.13 = f32[256,256]{0,1:T(8,128)} collective-permute-done((f32[256,256]{0,1:T(8,128)}, f32[256,256]{0,1:T(8,128)}, u32[]{:S(2)}, u32[]{:S(2)}) %collective-permute-start.13) | collective-permute-done | bytes 262176 | tf_op jit(solution)/shard_map/ppermute | solution.py:18
  155.2 6.6 %collective-permute-done.12 = f32[256,256]{0,1:T(8,128)} collective-permute-done((f32[256,256]{0,1:T(8,128)}, f32[256,256]{0,1:T(8,128)}, u32[]{:S(2)}, u32[]{:S(2)}) %collective-permute-start.12) | collective-permute-done | bytes 262176 | tf_op jit(solution)/shard_map/ppermute | solution.py:18
  161.9 1.4 fusion.23
  (53 shorter events, 11.8 us)
Async XLA Ops:
  7.2 31.8 %copy-start.5 = (s32[16]{0:T(128)S(1)}, s32[16]{0:T(128)}, u32[]{:S(2)}) copy-start(s32[16]{0:T(128)} %param.11) | copy-start | bytes 196
  7.2 33.4 %copy-start.4 = (bf16[256,512]{1,0:T(8,128)(2,1)S(1)}, bf16[256,512]{1,0:T(8,128)(2,1)}, u32[]{:S(2)}) copy-start(bf16[256,512]{1,0:T(8,128)(2,1)} %param.6) | copy-start | bytes 786436
  8.9 48.9 %collective-permute-start.6 = (bf16[256,256]{1,0:T(8,128)(2,1)S(1)}, bf16[256,256]{1,0:T(8,128)(2,1)S(1)}, u32[]{:S(2)}, u32[]{:S(2)}) collective-permute-start(bf16[256,256]{1,0:T(8,128)(2,1)S(1)} %constant_dynamic-update-slice_fusion), channel_id=1, source_target_pairs={{0,7},{1,8},{2,9},{3,10},{4,11},{5,12},{6,13},{7,14},{8,15},{9,16}... | collective-permute-start | bytes 393224 | tf_op jit(solution)/shard_map/ppermute | solution.py:18
  12.6 45.1 %collective-permute-start.5 = (bf16[256,256]{1,0:T(8,128)(2,1)S(1)}, bf16[256,256]{1,0:T(8,128)(2,1)S(1)}, u32[]{:S(2)}, u32[]{:S(2)}) collective-permute-start(bf16[256,256]{1,0:T(8,128)(2,1)S(1)} %constant_dynamic-update-slice_fusion), channel_id=1, source_target_pairs={{0,6},{1,7},{2,8},{3,9},{4,10},{5,11},{6,12},{7,13},{8,14},{9,15},... | collective-permute-start | bytes 393224 | tf_op jit(solution)/shard_map/ppermute | solution.py:18
  17.3 40.4 %collective-permute-start.4 = (bf16[256,256]{1,0:T(8,128)(2,1)S(1)}, bf16[256,256]{1,0:T(8,128)(2,1)S(1)}, u32[]{:S(2)}, u32[]{:S(2)}) collective-permute-start(bf16[256,256]{1,0:T(8,128)(2,1)S(1)} %constant_dynamic-update-slice_fusion), channel_id=1, source_target_pairs={{0,5},{1,6},{2,7},{3,8},{4,9},{5,10},{6,11},{7,12},{8,13},{9,14},{... | collective-permute-start | bytes 393224 | tf_op jit(solution)/shard_map/ppermute | solution.py:18
  21.3 36.5 %collective-permute-start.3 = (bf16[256,256]{1,0:T(8,128)(2,1)S(1)}, bf16[256,256]{1,0:T(8,128)(2,1)S(1)}, u32[]{:S(2)}, u32[]{:S(2)}) collective-permute-start(bf16[256,256]{1,0:T(8,128)(2,1)S(1)} %constant_dynamic-update-slice_fusion), channel_id=1, source_target_pairs={{0,4},{1,5},{2,6},{3,7},{4,8},{5,9},{6,10},{7,11},{8,12},{9,13},{1... | collective-permute-start | bytes 393224 | tf_op jit(solution)/shard_map/ppermute | solution.py:18
  27.3 13.4 %collective-permute-start = (bf16[256,256]{1,0:T(8,128)(2,1)S(1)}, bf16[256,256]{1,0:T(8,128)(2,1)S(1)}, u32[]{:S(2)}, u32[]{:S(2)}) collective-permute-start(bf16[256,256]{1,0:T(8,128)(2,1)S(1)} %constant_dynamic-update-slice_fusion), channel_id=1, source_target_pairs={{0,1},{1,2},{2,3},{3,4},{4,5},{5,6},{6,7},{7,8},{8,9},{9,10},{10,1... | collective-permute-start | bytes 393224 | tf_op jit(solution)/shard_map/ppermute | solution.py:18
  31.7 59.8 %all-to-all-start = ((bf16[8,512,256]{2,1,0:T(8,128)(2,1)}), bf16[8,512,256]{2,1,0:T(8,128)(2,1)S(1)}, u32[]{:S(2)}, u32[]{:S(2)}) async-start(bf16[8,512,256]{2,1,0:T(8,128)(2,1)} %stack.2), calls=%async_computation.1 | async-start | bytes 4194304 | tf_op jit(solution)/shard_map/all_to_all | solution.py:12
  38.8 125.9 %reduce-scatter.2.cloned.1.call-start = ((), (), s32[]{:S(2)}) async-start(), calls=%async_computation.2 | async-start | bytes 4718592 | tf_op jit(solution)/shard_map/reduce_scatter | solution.py:61
  40.7 23.1 %copy-start.2 = (bf16[256,512]{0,1:T(8,128)(2,1)}, bf16[256,512]{0,1:T(8,128)(2,1)S(1)}, u32[]{:S(2)}) copy-start(bf16[256,512]{0,1:T(8,128)(2,1)S(1)} %copy.75) | copy-start | bytes 786436
  40.8 7.9 %collective-permute-start.1 = (bf16[256,256]{1,0:T(8,128)(2,1)S(1)}, bf16[256,256]{1,0:T(8,128)(2,1)S(1)}, u32[]{:S(2)}, u32[]{:S(2)}) collective-permute-start(bf16[256,256]{1,0:T(8,128)(2,1)S(1)} %constant_dynamic-update-slice_fusion), channel_id=1, source_target_pairs={{0,2},{1,3},{2,4},{3,5},{4,6},{5,7},{6,8},{7,9},{8,10},{9,11},{10,... | collective-permute-start | bytes 393224 | tf_op jit(solution)/shard_map/ppermute | solution.py:18
  48.7 9.0 %collective-permute-start.2 = (bf16[256,256]{1,0:T(8,128)(2,1)S(1)}, bf16[256,256]{1,0:T(8,128)(2,1)S(1)}, u32[]{:S(2)}, u32[]{:S(2)}) collective-permute-start(bf16[256,256]{1,0:T(8,128)(2,1)S(1)} %constant_dynamic-update-slice_fusion), channel_id=1, source_target_pairs={{0,3},{1,4},{2,5},{3,6},{4,7},{5,8},{6,9},{7,10},{8,11},{9,12},{10... | collective-permute-start | bytes 393224 | tf_op jit(solution)/shard_map/ppermute | solution.py:18
  91.4 3.6 %copy-start = (bf16[4,256,2048]{1,2,0:T(8,128)(2,1)S(1)}, bf16[4,256,2048]{1,2,0:T(8,128)(2,1)}, u32[]{:S(2)}) copy-start(bf16[4,256,2048]{1,2,0:T(8,128)(2,1)} %fusion.5) | copy-start | bytes 12582916
  95.0 2.2 %copy-start.1 = (bf16[512,4096]{1,0:T(8,128)(2,1)S(1)}, bf16[512,4096]{1,0:T(8,128)(2,1)}, u32[]{:S(2)}) copy-start(bf16[512,4096]{1,0:T(8,128)(2,1)} %param.9) | copy-start | bytes 12582916
  104.2 4.4 %copy-start.3 = (bf16[256,512]{0,1:T(8,128)(2,1)S(1)}, bf16[256,512]{0,1:T(8,128)(2,1)}, u32[]{:S(2)}) copy-start(bf16[256,512]{0,1:T(8,128)(2,1)} %copy-done.2) | copy-start | bytes 786436
  111.1 11.7 %collective-permute-start.7 = (f32[256,256]{0,1:T(8,128)S(1)}, f32[256,256]{0,1:T(8,128)S(1)}, u32[]{:S(2)}, u32[]{:S(2)}) collective-permute-start(f32[256,256]{0,1:T(8,128)S(1)} %get-tuple-element.16), channel_id=1, source_target_pairs={{1,0},{2,1},{3,2},{4,3},{5,4},{6,5},{7,6},{8,7},{9,8},{10,9},{11,1... | collective-permute-start | bytes 786440 | tf_op jit(solution)/shard_map/ppermute | solution.py:18
  113.1 12.7 %collective-permute-start.8 = (f32[256,256]{0,1:T(8,128)S(1)}, f32[256,256]{0,1:T(8,128)S(1)}, u32[]{:S(2)}, u32[]{:S(2)}) collective-permute-start(f32[256,256]{0,1:T(8,128)S(1)} %get-tuple-element.17), channel_id=1, source_target_pairs={{2,0},{3,1},{4,2},{5,3},{6,4},{7,5},{8,6},{9,7},{10,8},{11,9},{12,... | collective-permute-start | bytes 786440 | tf_op jit(solution)/shard_map/ppermute | solution.py:18
  116.5 12.8 %collective-permute-start.9 = (f32[256,256]{0,1:T(8,128)}, f32[256,256]{0,1:T(8,128)}, u32[]{:S(2)}, u32[]{:S(2)}) collective-permute-start(f32[256,256]{0,1:T(8,128)} %get-tuple-element.18), channel_id=1, source_target_pairs={{3,0},{4,1},{5,2},{6,3},{7,4},{8,5},{9,6},{10,7},{11,8},{12,9},{13... | collective-permute-start | bytes 786440 | tf_op jit(solution)/shard_map/ppermute | solution.py:18
  118.4 19.7 %collective-permute-start.10 = (f32[256,256]{0,1:T(8,128)}, f32[256,256]{0,1:T(8,128)}, u32[]{:S(2)}, u32[]{:S(2)}) collective-permute-start(f32[256,256]{0,1:T(8,128)} %get-tuple-element.19), channel_id=1, source_target_pairs={{4,0},{5,1},{6,2},{7,3},{8,4},{9,5},{10,6},{11,7},{12,8},{13,9},{1... | collective-permute-start | bytes 786440 | tf_op jit(solution)/shard_map/ppermute | solution.py:18
  120.9 22.2 %collective-permute-start.11 = (f32[256,256]{0,1:T(8,128)}, f32[256,256]{0,1:T(8,128)}, u32[]{:S(2)}, u32[]{:S(2)}) collective-permute-start(f32[256,256]{0,1:T(8,128)} %get-tuple-element.20), channel_id=1, source_target_pairs={{5,0},{6,1},{7,2},{8,3},{9,4},{10,5},{11,6},{12,7},{13,8},{14,9},{... | collective-permute-start | bytes 786440 | tf_op jit(solution)/shard_map/ppermute | solution.py:18
  122.9 32.3 %collective-permute-start.13 = (f32[256,256]{0,1:T(8,128)}, f32[256,256]{0,1:T(8,128)}, u32[]{:S(2)}, u32[]{:S(2)}) collective-permute-start(f32[256,256]{0,1:T(8,128)} %get-tuple-element.21), channel_id=1, source_target_pairs={{7,0},{8,1},{9,2},{10,3},{11,4},{12,5},{13,6},{14,7},{15,8},{16,9}... | collective-permute-start | bytes 786440 | tf_op jit(solution)/shard_map/ppermute | solution.py:18
  125.7 36.1 %collective-permute-start.12 = (f32[256,256]{0,1:T(8,128)}, f32[256,256]{0,1:T(8,128)}, u32[]{:S(2)}, u32[]{:S(2)}) collective-permute-start(f32[256,256]{0,1:T(8,128)} %get-tuple-element.22), channel_id=1, source_target_pairs={{6,0},{7,1},{8,2},{9,3},{10,4},{11,5},{12,6},{13,7},{14,8},{15,9},... | collective-permute-start | bytes 786440 | tf_op jit(solution)/shard_map/ppermute | solution.py:18
Sparse Core Ops, SparseCore 0:
  100.7 52.6 reduce-scatter.1
